TPU v7x, 512 devices: a whole 4x8x8 slice. The times are simulated.
512 devices in a mesh: req: 64 (over z, x, core), tp: 8 (over y).
Axes of the slice: x: 4, y: 8, z: 8, core: 2. Of those that a mesh axis runs over, the one named last changes fastest.
Arguments:
- q_new: bfloat16 [4096, 5120], P('req', 'tp'), may hold values from -6 to 6
- k_new: bfloat16 [4096, 1024], P('req', 'tp'), may hold values from -15 to 15
- v_new: bfloat16 [4096, 1024], P('req', 'tp'), may hold values from -6 to 6
- k_cache: bfloat16 [1024, 128, 1024], P('req', None, 'tp'), may hold values from -16 to 16
- v_cache: bfloat16 [1024, 128, 1024], P('req', None, 'tp'), may hold values from -6 to 6
- lengths: int32 [32], replicated, may hold values from 1 to 4096, as said below
- page_table: int32 [32, 32], replicated, may hold values from -1 to 1023, as said below
- w_out: bfloat16 [5120, 5120], P('req', 'tp'), may hold values from -0.078125 to 0.078125
Outputs:
- attn_out: bfloat16 [4096, 5120], P('req')
Inputs may be any that keep to these rules, and one draw needn't show every extreme that they name: `lengths`: the last request, 31, has exactly 4096 cached tokens; every request has at least one. `page_table`: request r uses ceil(lengths[r] / 128) logical pages. Its first ceil(ceil(lengths[r] / 128) / 2) logical pages lie among global pages 2r * 16 to (2r + 1) * 16 - 1, the rest among (2r + 1) * 16 to (2r + 2) * 16 - 1; distinct logical pages use distinct global pages; entries past a request's last page are -1.
All inputs are finite; a program needn't handle non-finite values.
Results may differ from a plain program's by a relative error of at most 0.024.
Values may be sent and summed in bfloat16 or wider, within the bound.
No kernel may reach another device: no remote copies, remote signals or barrier semaphores. Data moves between devices by JAX's collectives and lax.ppermute only.
A program may use at most 64 MiB of HBM per device.

v0:
```python
import math
import jax
import jax.numpy as jnp
from jax import lax
from jax.sharding import Mesh
from jax.sharding import PartitionSpec as P

HD = 128
GROUP = 5
ROWS = ("z", "x", "core")
ROPE_BASE = 1000000.0
FLOOR_SCORE = -1e30


def from_partner(value, axis, distance):
    return lax.ppermute(value, axis, [(i, i ^ 1 << distance) for i in range(lax.axis_size(axis))])


def rotate(values, places):
    inverse = 1.0 / ROPE_BASE ** (jnp.arange(0, HD, 2).astype(jnp.float32) / HD)
    angles = places.astype(jnp.float32)[:, None] * inverse[None, :]
    cosine = jnp.concatenate([jnp.cos(angles), jnp.cos(angles)], axis=-1)[:, None, :]
    sine = jnp.concatenate([jnp.sin(angles), jnp.sin(angles)], axis=-1)[:, None, :]
    first_half = values[..., : HD // 2]
    second_half = values[..., HD // 2 :]
    turned = jnp.concatenate([-second_half, first_half], axis=-1)
    return values * cosine + turned * sine


def absorb(state, queries, block_keys, block_values, allowed, scale):
    running_max, running_sum, output = state
    scores = (
        jnp.einsum("qcgd,kcd->cgqk", queries, block_keys, preferred_element_type=jnp.float32)
        * scale
    )
    scores = jnp.where(allowed[None, None], scores, FLOOR_SCORE)
    new_max = jnp.maximum(running_max, jnp.max(scores, axis=-1))
    factor = jnp.exp(running_max - new_max)
    weights = jnp.where(allowed[None, None], jnp.exp(scores - new_max[..., None]), 0.0)
    running_sum = running_sum * factor + jnp.sum(weights, axis=-1)
    mixed = jnp.einsum(
        "cgqk,kcd->qcgd",
        weights.astype(jnp.bfloat16),
        block_values,
        preferred_element_type=jnp.float32,
    )
    output = output * jnp.transpose(factor, (2, 0, 1))[..., None] + mixed
    return (new_max, running_sum, output)


def output_rows(w_out):
    parts = lax.axis_size("tp")
    rows, width = w_out.shape
    share = rows // parts
    pieces = lax.all_to_all(w_out.reshape(parts, share, width), "tp", 0, 0, tiled=True)
    mine = jnp.transpose(pieces, (1, 0, 2))
    near = lax.all_gather(mine, "z", axis=0, tiled=True)
    return (lax.all_gather(near, ("x", "core"), axis=0, tiled=True), share)


def shards(q_new, k_new, v_new, k_cache, v_cache, lengths, page_table, w_out):
    own_rows = q_new.shape[0]
    all_rows = 2 * own_rows
    local_heads = k_new.shape[1] // HD
    pages_local = k_cache.shape[0]
    page_rows = k_cache.shape[1]
    scale = 1.0 / math.sqrt(HD)
    weights_mine, share = output_rows(w_out)
    device_row = (lax.axis_index("z") * lax.axis_size("x") + lax.axis_index("x")) * lax.axis_size(
        "core"
    ) + lax.axis_index("core")
    parity = device_row % 2
    request = device_row // 2
    length = lengths[request]
    own_places = length + parity * own_rows + jnp.arange(own_rows)
    own_queries = rotate(
        q_new.reshape(own_rows, local_heads * GROUP, HD).astype(jnp.float32), own_places
    ).astype(jnp.bfloat16)
    own_keys = rotate(
        k_new.reshape(own_rows, local_heads, HD).astype(jnp.float32), own_places
    ).astype(jnp.bfloat16)
    own_values = v_new.reshape(own_rows, local_heads, HD)
    query_heads = own_queries.shape[1]
    peer_pack = from_partner(
        jnp.concatenate([own_queries, own_keys, own_values], axis=1), "core", 0
    )
    peer_queries = peer_pack[:, :query_heads]
    peer_keys = peer_pack[:, query_heads : query_heads + local_heads]
    peer_values = peer_pack[:, query_heads + local_heads :]

    def ordered(mine, theirs):
        return jnp.where(
            parity == 0,
            jnp.concatenate([mine, theirs], axis=0),
            jnp.concatenate([theirs, mine], axis=0),
        )

    queries = ordered(own_queries, peer_queries).reshape(all_rows, local_heads, GROUP, HD)
    fresh_keys = ordered(own_keys, peer_keys)
    fresh_values = ordered(own_values, peer_values)
    state = (
        jnp.full((local_heads, GROUP, all_rows), FLOOR_SCORE, jnp.float32),
        jnp.zeros((local_heads, GROUP, all_rows), jnp.float32),
        jnp.zeros((all_rows, local_heads, GROUP, HD), jnp.float32),
    )
    token_index = jnp.arange(all_rows)
    causal = (token_index[None, :] <= token_index[:, None]) & (parity == 1)
    state = absorb(state, queries, fresh_keys, fresh_values, causal, scale)
    page_count = (length + page_rows - 1) // page_rows
    even_pages = (page_count + 1) // 2
    first_page = jnp.where(parity == 0, 0, even_pages)
    last_page = jnp.where(parity == 0, even_pages, page_count)
    table_row = page_table[request]
    logical = jnp.arange(table_row.shape[0])
    in_range = (logical >= first_page) & (logical < last_page)
    offset = device_row * pages_local
    slot_ids = jnp.arange(pages_local)
    match = in_range[:, None] & (table_row[:, None] - offset == slot_ids[None, :])
    used = jnp.any(match, axis=0)
    base = jnp.sum(jnp.where(match, logical[:, None], 0), axis=0) * page_rows
    key_places = (base[:, None] + jnp.arange(page_rows)[None, :]).reshape(-1)
    usable = jnp.repeat(used, page_rows) & (key_places < length)
    allowed = jnp.broadcast_to(usable[None, :], (all_rows, pages_local * page_rows))
    pool_keys = k_cache.reshape(pages_local * page_rows, local_heads, HD)
    pool_values = v_cache.reshape(pages_local * page_rows, local_heads, HD)
    half = pool_keys.shape[0] // 2
    for start in (0, half):
        state = absorb(
            state,
            queries,
            pool_keys[start : start + half],
            pool_values[start : start + half],
            allowed[:, start : start + half],
            scale,
        )
    running_max, running_sum, output = state
    peer_start = (1 - parity) * own_rows
    own_start = parity * own_rows
    outgoing = (
        lax.dynamic_slice_in_dim(output, peer_start, own_rows, 0),
        lax.dynamic_slice_in_dim(running_max, peer_start, own_rows, 2),
        lax.dynamic_slice_in_dim(running_sum, peer_start, own_rows, 2),
    )
    outgoing = jnp.concatenate(
        [
            outgoing[0].astype(jnp.bfloat16),
            jnp.transpose(outgoing[1], (2, 0, 1))[..., None].astype(jnp.bfloat16),
            jnp.transpose(outgoing[2], (2, 0, 1))[..., None].astype(jnp.bfloat16),
        ],
        axis=-1,
    )
    incoming = from_partner(outgoing, "core", 0).astype(jnp.float32)
    other_output = incoming[..., :HD]
    other_max = jnp.transpose(incoming[..., HD], (1, 2, 0))
    other_sum = jnp.transpose(incoming[..., HD + 1], (1, 2, 0))
    mine_output = lax.dynamic_slice_in_dim(output, own_start, own_rows, 0)
    mine_max = lax.dynamic_slice_in_dim(running_max, own_start, own_rows, 2)
    mine_sum = lax.dynamic_slice_in_dim(running_sum, own_start, own_rows, 2)
    joint_max = jnp.maximum(mine_max, other_max)
    mine_factor = jnp.exp(mine_max - joint_max)
    other_factor = jnp.exp(other_max - joint_max)
    joint_sum = mine_sum * mine_factor + other_sum * other_factor
    joint_output = (
        mine_output * jnp.transpose(mine_factor, (2, 0, 1))[..., None]
        + other_output * jnp.transpose(other_factor, (2, 0, 1))[..., None]
    )
    attention = (
        (joint_output / jnp.transpose(joint_sum, (2, 0, 1))[..., None])
        .reshape(own_rows, local_heads * GROUP * HD)
        .astype(jnp.bfloat16)
    )
    full_rows = lax.all_gather(attention[:, None], "tp", axis=1, tiled=True)
    projected = lax.dot_general(
        full_rows, weights_mine, (((1, 2), (1, 2)), ((), ())), preferred_element_type=jnp.float32
    )
    depth = lax.axis_size("z")
    projected = projected.reshape(own_rows, -1, depth, share)
    projected = jnp.transpose(projected, (0, 2, 1, 3)).reshape(own_rows, -1, share)
    projected = projected.astype(jnp.bfloat16)
    gathered = lax.all_gather(projected, "tp", axis=2, tiled=True)
    return gathered.reshape(own_rows, -1)


def solution(mesh):
    in_specs = (
        P(ROWS, "tp"),
        P(ROWS, "tp"),
        P(ROWS, "tp"),
        P(ROWS, None, "tp"),
        P(ROWS, None, "tp"),
        P(),
        P(),
        P(ROWS, "tp"),
    )
    out_specs = P(ROWS, None)
    rows, parts = mesh.devices.shape
    cores = 2
    depth = 4 if rows % (4 * cores) == 0 else 1
    split = Mesh(mesh.devices.reshape(depth, rows // (depth * cores), cores, parts), ROWS + ("tp",))
    return jax.shard_map(
        shards, mesh=split, in_specs=in_specs, out_specs=out_specs, check_vma=False
    )
```

profile of v0, /device:TPU:6, one launch (start us, length us, event | category | flops | bytes accessed | tf_op | source)
XLA Modules:
  0.0 135.1 jit_solution(9151260461402743674)
XLA Ops:
  6.5 0.0 all-gather.2.cloned.1.call-start
  6.6 1.0 reshape.452
  7.6 16.7 %all_to_all.5 = bf16[8,10,640]{2,1,0:T(8,128)(2,1)S(1)} all-to-all(bf16[8,10,640]{2,1,0:T(8,128)(2,1)S(1)} %reshape.452), channel_id=1, replica_groups=mesh['z'=4,'x'=8,'core'=2,'tp'=8] {'tp'}, dimensions={0} | all-to-all | bytes 204800 | tf_op jit(solution)/shard_map/all_to_all | solution.py:55
  24.3 21.0 %all_gather.13 = bf16[40,8,640]{2,1,0:T(8,128)(2,1)S(1)} all-gather(bf16[10,8,640]{2,1,0:T(8,128)(2,1)S(1)} %copy.92), channel_id=1, replica_groups=mesh['z'=4,'x'=8,'core'=2,'tp'=8] {'z'}, dimensions={0}, use_global_device_ids=true | all-gather | bytes 512000 | tf_op jit(solution)/shard_map/all_gather | solution.py:57
  45.3 0.8 copy.93
  46.1 0.1 reshape.454
  46.2 0.6 dynamic_slice.24
  47.5 0.2 multiply_cosine_fusion
  47.7 0.1 fusion.54
  47.8 0.1 pad_maximum_fusion.2
  48.0 0.1 slice_negate_fusion
  48.1 0.1 fusion.41
  48.3 0.1 pad_maximum_fusion.1
  48.4 1.9 %collective-permute-start = (bf16[64,7,128]{2,1,0:T(8,128)(2,1)S(1)}, bf16[64,7,128]{2,1,0:T(8,128)(2,1)S(1)}, u32[]{:S(2)}, u32[]{:S(2)}) collective-permute-start(bf16[64,7,128]{2,1,0:T(8,128)(2,1)S(1)} %pad_maximum_fusion.1), channel_id=1, source_target_pairs={{0,8},{8,0},{1,9},{9,1},{2,10},{10,2},{3,11},{11,3},{4,12},{12,4},... | collective-permute-start | bytes 344072 | tf_op jit(solution)/shard_map/ppermute | solution.py:16
  51.1 0.7 fusion.97
  51.8 0.1 fusion.77
  51.9 0.1 select_reduce_fusion
  52.0 0.7 fusion.79
  52.8 0.8 fusion.110
  53.6 0.1 fusion.112
  53.7 0.1 maximum_select_fusion
  53.9 0.2 fusion.113
  54.1 0.6 fusion.2
  54.7 0.6 fusion.3
  55.4 0.1 fusion.38
  55.4 1.5 %fusion.4 = (f32[5,128]{1,0:T(8,128)S(1)}, f32[5,128]{1,0:T(8,128)S(1)}) fusion(f32[128,5,1024]{2,0,1:T(8,128)S(1)} %get-tuple-element.38, f32[5,128]{1,0:T(8,128)S(1)} %get-tuple-element.10, pred[1024]{0:T(1024)(128)(4,1)S(1)} %get-tuple-element.8, f32[5,128]{1,0:T(8,128)S(1)} %get-tuple-element.9, f32[128,5,1024]{2,0,1:T(8,128)S(1)} %get-tuple-element.36, ...), kind=kLoop, calls=%fused_computation.8 | loop fusion | flops 6552320 | bytes 5255168 | tf_op jit(solution)/shard_map/reduce_sum | solution.py:40
  57.0 0.1 fusion.90
  57.0 0.1 copy.87
  57.2 0.1 fusion.91
  57.3 0.1 copy.88
  57.4 0.3 fusion.35
  57.7 2.5 %fusion.31 = f32[128,1,5,128]{3,0,2,1:T(8,128)S(1)} fusion(f32[128,1,5,128]{3,0,2,1:T(8,128)S(1)} %fusion.35, bf16[1024,128,1]{1,0,2:T(8,128)(2,1)} %bitcast.311, f32[128,5,1024]{2,0,1:T(8,128)} %copy-done, f32[5,128]{1,0:T(8,128)S(1)} %get-tuple-element.10, pred[1024]{0:T(1024)(128)(4,1)S(1)} %get-tuple-element.8, f32[128,5]{0,1:T(8,128)S(1)} %get-tuple-element.24), kind=kOutput, calls=%fused_computation.27 | convolution fusion | flops 171212800 | bytes 3545088 | tf_op jit(solution)/shard_map/cgqk,kcd->qcgd/dot_general | solution.py:41
  60.2 0.7 fusion.28
  61.0 0.1 pad_maximum_fusion
  61.1 2.4 %collective-permute-start.1 = (bf16[64,1,5,130]{3,0,2,1:T(8,128)(2,1)S(1)}, bf16[64,1,5,130]{3,0,2,1:T(8,128)(2,1)S(1)}, u32[]{:S(2)}, u32[]{:S(2)}) collective-permute-start(bf16[64,1,5,130]{3,0,2,1:T(8,128)(2,1)S(1)} %pad_maximum_fusion), channel_id=1, source_target_pairs={{0,8},{8,0},{1,9},{9,1},{2,10},{10,2},{3,11},{11,3},{4,12},{12,4},... | collective-permute-start | bytes 249608 | tf_op jit(solution)/shard_map/ppermute | solution.py:16
  63.5 1.0 collective-permute-done.1
  64.5 0.2 slice_reduce_fusion.1
  64.8 0.1 fusion.95
  64.8 0.2 copy_bitcast_fusion
  65.1 25.7 %all_gather.12 = bf16[64,8,640]{2,0,1:T(8,128)(2,1)S(1)} all-gather(bf16[64,1,640]{2,0,1:T(8,128)(2,1)S(1)} %copy_bitcast_fusion), channel_id=1, replica_groups=mesh['z'=4,'x'=8,'core'=2,'tp'=8] {'tp'}, dimensions={1}, use_global_device_ids=true | all-gather | bytes 737280 | tf_op jit(solution)/shard_map/all_gather | solution.py:172
  90.7 4.9 %fusion.37 = bf16[64,640]{1,0:T(8,128)(2,1)S(1)} fusion(bf16[64,8,640]{2,0,1:T(8,128)(2,1)S(1)} %all_gather.12, bf16[640,8,640]{2,0,1:T(8,128)(2,1)} %all-gather.2.cloned.1.call-done), kind=kOutput, calls=%fused_computation.32 | convolution fusion | flops 419471360 | bytes 7290880 | tf_op jit(solution)/shard_map/dot_general | solution.py:173
  95.7 0.2 copy.94
  95.8 0.1 convert_element_type.134
  95.9 0.1 copy.95
  96.0 0.1 copy.96
  96.2 27.6 %all_gather.15 = bf16[64,64,80]{1,0,2:T(8,128)(2,1)S(1)} all-gather(bf16[64,64,10]{1,0,2:T(8,128)(2,1)S(1)} %copy.96), channel_id=1, replica_groups=mesh['z'=4,'x'=8,'core'=2,'tp'=8] {'tp'}, dimensions={2}, use_global_device_ids=true | all-gather | bytes 737280 | tf_op jit(solution)/shard_map/all_gather | solution.py:180
  123.8 1.5 %copy.97 = bf16[64,64,80]{2,1,0:T(8,128)(2,1)S(1)} copy(bf16[64,64,80]{1,0,2:T(8,128)(2,1)S(1)} %all_gather.15) | data formatting | bytes 1310720 | tf_op jit(solution)/shard_map/all_gather | solution.py:180
  125.3 2.9 %reshape.453 = bf16[64,5120]{1,0:T(8,128)(2,1)} reshape(bf16[64,64,80]{2,1,0:T(8,128)(2,1)S(1)} %copy.97) | data formatting | bytes 1310720 | tf_op jit(solution)/shard_map/reshape | solution.py:181
  (35 shorter events, 0.3 us)
Async XLA Ops:
  6.5 39.6 %copy-start.3 = (bf16[64,640]{1,0:T(8,128)(2,1)S(1)}, bf16[64,640]{1,0:T(8,128)(2,1)}, u32[]{:S(2)}) copy-start(bf16[64,640]{1,0:T(8,128)(2,1)} %param.8) | copy-start | bytes 245764
  6.5 39.7 %copy-start.6 = (s32[32]{0:T(128)S(1)}, s32[32]{0:T(128)}, u32[]{:S(2)}) copy-start(s32[32]{0:T(128)} %param.13) | copy-start | bytes 388
  6.5 41.0 %copy-start.4 = (bf16[64,128]{1,0:T(8,128)(2,1)S(1)}, bf16[64,128]{1,0:T(8,128)(2,1)}, u32[]{:S(2)}) copy-start(bf16[64,128]{1,0:T(8,128)(2,1)} %param.9) | copy-start | bytes 49156
  6.5 41.4 %copy-start.5 = (bf16[64,128]{1,0:T(8,128)(2,1)S(1)}, bf16[64,128]{1,0:T(8,128)(2,1)}, u32[]{:S(2)}) copy-start(bf16[64,128]{1,0:T(8,128)(2,1)} %param.10) | copy-start | bytes 49156
  6.5 84.2 %all-gather.2.cloned.1.call-start = ((), (), s32[]{:S(2)}) async-start(), calls=%async_computation.1 | async-start | bytes 6963200 | tf_op jit(solution)/shard_map/all_gather | solution.py:58
  24.2 28.5 %copy-start.1 = (bf16[16,128,128]{2,1,0:T(8,128)(2,1)S(1)}, bf16[16,128,128]{2,1,0:T(8,128)(2,1)}, u32[]{:S(2)}) copy-start(bf16[16,128,128]{2,1,0:T(8,128)(2,1)} %param.11) | copy-start | bytes 1572868
  46.0 6.7 %copy-start.2 = (bf16[16,128,128]{2,1,0:T(8,128)(2,1)S(1)}, bf16[16,128,128]{2,1,0:T(8,128)(2,1)}, u32[]{:S(2)}) copy-start(bf16[16,128,128]{2,1,0:T(8,128)(2,1)} %param.12) | copy-start | bytes 1572868
  48.4 5.2 %collective-permute-start = (bf16[64,7,128]{2,1,0:T(8,128)(2,1)S(1)}, bf16[64,7,128]{2,1,0:T(8,128)(2,1)S(1)}, u32[]{:S(2)}, u32[]{:S(2)}) collective-permute-start(bf16[64,7,128]{2,1,0:T(8,128)(2,1)S(1)} %pad_maximum_fusion.1), channel_id=1, source_target_pairs={{0,8},{8,0},{1,9},{9,1},{2,10},{10,2},{3,11},{11,3},{4,12},{12,4},... | collective-permute-start | bytes 344072 | tf_op jit(solution)/shard_map/ppermute | solution.py:16
  54.7 2.2 %copy-start = (f32[128,5,1024]{2,0,1:T(8,128)}, f32[128,5,1024]{2,0,1:T(8,128)S(1)}, u32[]{:S(2)}) copy-start(f32[128,5,1024]{2,0,1:T(8,128)S(1)} %get-tuple-element.38) | copy-start | bytes 7864324
  61.1 3.4 %collective-permute-start.1 = (bf16[64,1,5,130]{3,0,2,1:T(8,128)(2,1)S(1)}, bf16[64,1,5,130]{3,0,2,1:T(8,128)(2,1)S(1)}, u32[]{:S(2)}, u32[]{:S(2)}) collective-permute-start(bf16[64,1,5,130]{3,0,2,1:T(8,128)(2,1)S(1)} %pad_maximum_fusion), channel_id=1, source_target_pairs={{0,8},{8,0},{1,9},{9,1},{2,10},{10,2},{3,11},{11,3},{4,12},{12,4},... | collective-permute-start | bytes 249608 | tf_op jit(solution)/shard_map/ppermute | solution.py:16
Sparse Core Ops, SparseCore 0:
  46.2 43.5 all-gather.1
where the time goes:
time: 135 us
  blocking collectives  90.9 us (67%)
  between operations  15.1 us (11%)
  matrix products  9.93 us (7%)
  local copies, waits for them, and re-layouts  9.09 us (7%)
  other arithmetic  4.56 us (3%)
  starting transfers between devices  4.38 us (3%)
    all_gather x1, blocking collectives, shards(): gathered = lax.all_gather(projected, 'tp', axis=2, tiled=True)  27.6 us
    all_gather x1, blocking collectives, shards(): full_rows = lax.all_gather(attention[:, None], 'tp', axis=1, tiled=True)  25.7 us
    all_gather x1, blocking collectives, output_rows(): near = lax.all_gather(mine, 'z', axis=0, tiled=True)  21 us
    all_to_all x1, blocking collectives, output_rows(): lax.all_to_all(w_out.reshape(parts, share, width), 'tp', 0, 0, tiled=True)  16.7 us
    dot_general x1, matrix products, shards(): lax.dot_general(full_rows, weights_mine, (((1, 2), (1, 2)), ((), ())), pr...  4.94 us
    ppermute x2, starting transfers between devices, from_partner(): lax.ppermute(value, axis, [(i, i ^ 1 << distance) for i in range(lax.axis...  4.35 us
    dot_general x3, matrix products, absorb(): jnp.einsum('cgqk,kcd->qcgd', weights.astype(jnp.bfloat16), block_values,...  3.52 us
    reshape x1, local copies, waits for them, and re-layouts, shards(): return gathered.reshape(own_rows, -1)  2.92 us
  transfers between devices with their start and end apart: 3, of which 1 were waited for; matrix products, arithmetic and copies ran while one was open for 9% of the time, Pallas kernels for 0%

commit v1 on v0

--- a/solution.py
+++ b/solution.py
@@ -10,6 +10,28 @@
 ROWS = ("z", "x", "core")
 ROPE_BASE = 1000000.0
 FLOOR_SCORE = -1e30
+
+
+def laid_out(blocks, dim):
+    blocks = jnp.moveaxis(blocks, 0, dim)
+    shape = blocks.shape
+    return blocks.reshape(*shape[:dim], shape[dim] * shape[dim + 1], *shape[dim + 2 :])
+
+
+def gather_around(array, axis, dim):
+    size = lax.axis_size(axis)
+    pairs = [(i, (i + 1) % size) for i in range(size)]
+    back = [(b, a) for a, b in pairs]
+    lower, upper = ([], [])
+    for hop in range(size - 1):
+        if hop % 2 == 0:
+            lower.append(lax.ppermute(lower[-1] if lower else array, axis, pairs))
+        else:
+            upper.append(lax.ppermute(upper[-1] if upper else array, axis, back))
+    tiles = jnp.stack([*lower[::-1], array, *upper])
+    shift = lax.axis_index(axis) - len(lower)
+    tiles = tiles[(jnp.arange(size) - shift) % size]
+    return laid_out(tiles, dim)
 
 
 def from_partner(value, axis, distance):
@@ -169,7 +191,7 @@
         .reshape(own_rows, local_heads * GROUP * HD)
         .astype(jnp.bfloat16)
     )
-    full_rows = lax.all_gather(attention[:, None], "tp", axis=1, tiled=True)
+    full_rows = gather_around(attention[:, None], "tp", 1)
     projected = lax.dot_general(
         full_rows, weights_mine, (((1, 2), (1, 2)), ((), ())), preferred_element_type=jnp.float32
     )

time: 135 us -> 151 us (1.12); the launches traced: 135 us -> 149 us
  blocking collectives: 90.9 us -> 65.8 us
  starting transfers between devices: 4.38 us -> 28.2 us
  waiting for transfers between devices: 1.02 us -> 8.93 us
  matrix products: 9.93 us -> 14.8 us
    all_gather x1 -> x0, blocking collectives: 25.7 us -> none  [shards(): full_rows = lax.all_gather(attention[:, None], 'tp', axis=1, tiled=True)]
    ppermute x0 -> x7, starting transfers between devices: none -> 23.9 us  [the longest x3 15.6 us: gather_around(): upper.append(lax.ppermute(upper[-1] if upper else array, axis, back))]
    ppermute x0 -> x7, waiting for transfers between devices: none -> 7.89 us  [the longest x4 6.24 us: gather_around(): lower.append(lax.ppermute(lower[-1] if lower else array, axis, pairs))]
    dot_general x1, matrix products: 4.94 us -> 9.76 us  [shards(): lax.dot_general(full_rows, weights_mine, (((1, 2), (1, 2)), ((), ())), pr...]
  transfers between devices with their start and end apart: 3 -> 10, of which waited for: 1 -> 6; matrix products, arithmetic and copies ran while one was open for 9% -> 11% of each run, Pallas kernels for 0% -> 0%
where the time goes in v1:
time: 151 us; the launch traced here: 149 us
  blocking collectives  65.8 us (44%)
  starting transfers between devices  28.2 us (19%)
  between operations  15.2 us (10%)
  matrix products  14.8 us (10%)
  local copies, waits for them, and re-layouts  10.4 us (7%)
  waiting for transfers between devices  8.93 us (6%)
  other arithmetic  6.03 us (4%)
    all_gather x1, blocking collectives, shards(): gathered = lax.all_gather(projected, 'tp', axis=2, tiled=True)  27.9 us
    all_gather x1, blocking collectives, output_rows(): near = lax.all_gather(mine, 'z', axis=0, tiled=True)  21.3 us
    all_to_all x1, blocking collectives, output_rows(): lax.all_to_all(w_out.reshape(parts, share, width), 'tp', 0, 0, tiled=True)  16.7 us
    ppermute x3, starting transfers between devices, gather_around(): upper.append(lax.ppermute(upper[-1] if upper else array, axis, back))  15.6 us
    dot_general x1, matrix products, shards(): lax.dot_general(full_rows, weights_mine, (((1, 2), (1, 2)), ((), ())), pr...  9.76 us
    ppermute x4, starting transfers between devices, gather_around(): lower.append(lax.ppermute(lower[-1] if lower else array, axis, pairs))  8.3 us
    ppermute x4, waiting for transfers between devices, gather_around(): lower.append(lax.ppermute(lower[-1] if lower else array, axis, pairs))  6.24 us
    ppermute x2, starting transfers between devices, from_partner(): lax.ppermute(value, axis, [(i, i ^ 1 << distance) for i in range(lax.axis...  4.3 us
  transfers between devices with their start and end apart: 10, of which 6 were waited for; matrix products, arithmetic and copies ran while one was open for 11% of the time, Pallas kernels for 0%

profile of v1, /device:TPU:6, one launch (start us, length us, event | category | flops | bytes accessed | tf_op | source)
XLA Modules:
  0.0 149.4 jit_solution(15456673577761612774)
XLA Ops:
  6.5 1.0 reshape.516
  7.5 16.7 %all_to_all.5 = bf16[8,10,640]{2,1,0:T(8,128)(2,1)S(1)} all-to-all(bf16[8,10,640]{2,1,0:T(8,128)(2,1)S(1)} %reshape.516), channel_id=1, replica_groups=mesh['z'=4,'x'=8,'core'=2,'tp'=8] {'tp'}, dimensions={0} | all-to-all | bytes 204800 | tf_op jit(solution)/shard_map/all_to_all | solution.py:77
  24.2 21.3 %all_gather.9 = bf16[40,8,640]{2,1,0:T(8,128)(2,1)} all-gather(bf16[10,8,640]{2,1,0:T(8,128)(2,1)S(1)} %copy.119), channel_id=1, replica_groups=mesh['z'=4,'x'=8,'core'=2,'tp'=8] {'z'}, dimensions={0}, use_global_device_ids=true | all-gather | bytes 512000 | tf_op jit(solution)/shard_map/all_gather | solution.py:79
  45.6 1.0 reshape.518
  46.5 1.2 dynamic_slice.24
  48.5 0.7 convert_bitcast_fusion
  49.2 0.2 multiply_cosine_fusion
  49.5 0.8 pad_maximum_fusion.2
  50.4 0.1 slice_negate_fusion
  50.5 0.1 fusion.52
  50.7 0.1 pad_maximum_fusion.1
  50.8 1.9 %collective-permute-start = (bf16[64,7,128]{2,1,0:T(8,128)(2,1)S(1)}, bf16[64,7,128]{2,1,0:T(8,128)(2,1)S(1)}, u32[]{:S(2)}, u32[]{:S(2)}) collective-permute-start(bf16[64,7,128]{2,1,0:T(8,128)(2,1)S(1)} %pad_maximum_fusion.1), channel_id=1, source_target_pairs={{0,8},{8,0},{1,9},{9,1},{2,10},{10,2},{3,11},{11,3},{4,12},{12,4},... | collective-permute-start | bytes 344072 | tf_op jit(solution)/shard_map/ppermute | solution.py:38
  53.4 0.7 fusion.107
  54.1 0.1 fusion.87
  54.3 0.1 select_reduce_fusion
  54.4 0.7 fusion.89
  55.2 0.7 fusion.122
  56.1 0.1 maximum_select_fusion
  56.2 0.2 fusion.125
  56.5 0.6 fusion.4
  57.1 0.6 fusion.5
  57.8 1.5 fusion.6
  59.4 0.1 copy.113
  59.6 0.1 copy.114
  59.8 0.3 fusion.40
  60.1 2.5 %fusion.36 = f32[128,1,5,128]{3,0,2,1:T(8,128)S(1)} fusion(f32[128,1,5,128]{3,0,2,1:T(8,128)S(1)} %fusion.40, bf16[1024,128,1]{1,0,2:T(8,128)(2,1)} %bitcast.342, f32[128,5,1024]{2,0,1:T(8,128)} %copy-done, f32[5,128]{1,0:T(8,128)S(1)} %get-tuple-element.10, pred[1024]{0:T(1024)(128)(4,1)S(1)} %get-tuple-element.8, f32[128,5]{0,1:T(8,128)S(1)} %get-tuple-element.24), kind=kOutput, calls=%fused_computation.31 | convolution fusion | flops 171212800 | bytes 3545088 | tf_op jit(solution)/shard_map/cgqk,kcd->qcgd/dot_general | solution.py:63
  62.6 0.7 fusion.33
  63.5 2.4 %collective-permute-start.1 = (bf16[64,1,5,130]{3,0,2,1:T(8,128)(2,1)S(1)}, bf16[64,1,5,130]{3,0,2,1:T(8,128)(2,1)S(1)}, u32[]{:S(2)}, u32[]{:S(2)}) collective-permute-start(bf16[64,1,5,130]{3,0,2,1:T(8,128)(2,1)S(1)} %pad_maximum_fusion), channel_id=1, source_target_pairs={{0,8},{8,0},{1,9},{9,1},{2,10},{10,2},{3,11},{11,3},{4,12},{12,4},... | collective-permute-start | bytes 249608 | tf_op jit(solution)/shard_map/ppermute | solution.py:38
  65.9 1.0 collective-permute-done.1
  66.9 0.2 slice_reduce_fusion.1
  67.2 0.2 fusion.59
  67.4 2.6 %collective-permute-start.2 = (bf16[64,1,640]{2,0,1:T(8,128)(2,1)S(1)}, bf16[64,1,640]{2,0,1:T(8,128)(2,1)S(1)}, u32[]{:S(2)}, u32[]{:S(2)}) collective-permute-start(bf16[64,1,640]{2,0,1:T(8,128)(2,1)S(1)} %copy_bitcast_fusion), channel_id=1, source_target_pairs={{0,1},{1,2},{2,3},{3,4},{4,5},{5,6},{6,7},{7,0},{8,9},{9,10},{10,1... | collective-permute-start | bytes 245768 | tf_op jit(solution)/shard_map/ppermute | solution.py:28
  70.0 5.2 %collective-permute-done.2 = bf16[64,1,640]{2,0,1:T(8,128)(2,1)S(1)} collective-permute-done((bf16[64,1,640]{2,0,1:T(8,128)(2,1)S(1)}, bf16[64,1,640]{2,0,1:T(8,128)(2,1)S(1)}, u32[]{:S(2)}, u32[]{:S(2)}) %collective-permute-start.2) | collective-permute-done | bytes 81952 | tf_op jit(solution)/shard_map/ppermute | solution.py:28
  75.3 1.9 %collective-permute-start.3 = (bf16[64,1,640]{2,0,1:T(8,128)(2,1)S(1)}, bf16[64,1,640]{2,0,1:T(8,128)(2,1)S(1)}, u32[]{:S(2)}, u32[]{:S(2)}) collective-permute-start(bf16[64,1,640]{2,0,1:T(8,128)(2,1)S(1)} %collective-permute-done.2), channel_id=1, source_target_pairs={{0,1},{1,2},{2,3},{3,4},{4,5},{5,6},{6,7},{7,0},{8,9},{9,10},{10,1... | collective-permute-start | bytes 245768 | tf_op jit(solution)/shard_map/ppermute | solution.py:28
  77.2 5.1 %collective-permute-start.6 = (bf16[64,1,640]{2,0,1:T(8,128)(2,1)S(1)}, bf16[64,1,640]{2,0,1:T(8,128)(2,1)S(1)}, u32[]{:S(2)}, u32[]{:S(2)}) collective-permute-start(bf16[64,1,640]{2,0,1:T(8,128)(2,1)S(1)} %copy_bitcast_fusion), channel_id=1, source_target_pairs={{1,0},{2,1},{3,2},{4,3},{5,4},{6,5},{7,6},{0,7},{9,8},{10,9},{11,1... | collective-permute-start | bytes 245768 | tf_op jit(solution)/shard_map/ppermute | solution.py:30
  82.3 0.5 collective-permute-done.3
  82.8 1.9 %collective-permute-start.4 = (bf16[64,1,640]{2,0,1:T(8,128)(2,1)S(1)}, bf16[64,1,640]{2,0,1:T(8,128)(2,1)S(1)}, u32[]{:S(2)}, u32[]{:S(2)}) collective-permute-start(bf16[64,1,640]{2,0,1:T(8,128)(2,1)S(1)} %collective-permute-done.3), channel_id=1, source_target_pairs={{0,1},{1,2},{2,3},{3,4},{4,5},{5,6},{6,7},{7,0},{8,9},{9,10},{10,1... | collective-permute-start | bytes 245768 | tf_op jit(solution)/shard_map/ppermute | solution.py:28
  84.7 5.1 %collective-permute-start.7 = (bf16[64,1,640]{2,0,1:T(8,128)(2,1)S(1)}, bf16[64,1,640]{2,0,1:T(8,128)(2,1)S(1)}, u32[]{:S(2)}, u32[]{:S(2)}) collective-permute-start(bf16[64,1,640]{2,0,1:T(8,128)(2,1)S(1)} %collective-permute-done.6), channel_id=1, source_target_pairs={{1,0},{2,1},{3,2},{4,3},{5,4},{6,5},{7,6},{0,7},{9,8},{10,9},{11,1... | collective-permute-start | bytes 245768 | tf_op jit(solution)/shard_map/ppermute | solution.py:30
  89.9 0.4 collective-permute-done.4
  90.3 1.9 %collective-permute-start.5 = (bf16[64,1,640]{2,0,1:T(8,128)(2,1)S(1)}, bf16[64,1,640]{2,0,1:T(8,128)(2,1)S(1)}, u32[]{:S(2)}, u32[]{:S(2)}) collective-permute-start(bf16[64,1,640]{2,0,1:T(8,128)(2,1)S(1)} %collective-permute-done.4), channel_id=1, source_target_pairs={{0,1},{1,2},{2,3},{3,4},{4,5},{5,6},{6,7},{7,0},{8,9},{9,10},{10,1... | collective-permute-start | bytes 245768 | tf_op jit(solution)/shard_map/ppermute | solution.py:28
  92.5 5.3 %collective-permute-start.8 = (bf16[64,1,640]{2,0,1:T(8,128)(2,1)S(1)}, bf16[64,1,640]{2,0,1:T(8,128)(2,1)S(1)}, u32[]{:S(2)}, u32[]{:S(2)}) collective-permute-start(bf16[64,1,640]{2,0,1:T(8,128)(2,1)S(1)} %collective-permute-done.7), channel_id=1, source_target_pairs={{1,0},{2,1},{3,2},{4,3},{5,4},{6,5},{7,6},{0,7},{9,8},{10,9},{11,1... | collective-permute-start | bytes 245768 | tf_op jit(solution)/shard_map/ppermute | solution.py:30
  98.0 1.6 %collective-permute-done.8 = bf16[64,1,640]{2,0,1:T(8,128)(2,1)S(1)} collective-permute-done((bf16[64,1,640]{2,0,1:T(8,128)(2,1)S(1)}, bf16[64,1,640]{2,0,1:T(8,128)(2,1)S(1)}, u32[]{:S(2)}, u32[]{:S(2)}) %collective-permute-start.8) | collective-permute-done | bytes 81952 | tf_op jit(solution)/shard_map/ppermute | solution.py:30
  99.6 0.7 gather_fusion
  100.3 9.8 %fusion.45 = bf16[64,4,16,10]{0,2,3,1:T(8,128)(2,1)S(1)} fusion(bf16[16,4,10,8,640]{4,3,2,1,0:T(8,128)(2,1)} %bitcast.348, bf16[8,64,640]{2,1,0:T(8,128)(2,1)S(1)} %gather_fusion), kind=kOutput, calls=%fused_computation.36 | convolution fusion | flops 419471360 | bytes 7290880 | tf_op jit(solution)/shard_map/dot_general | solution.py:195
  110.1 0.1 copy.122
  110.3 27.9 %all_gather.11 = bf16[64,64,80]{1,0,2:T(8,128)(2,1)S(1)} all-gather(bf16[64,64,10]{1,0,2:T(8,128)(2,1)S(1)} %copy.122), channel_id=1, replica_groups=mesh['z'=4,'x'=8,'core'=2,'tp'=8] {'tp'}, dimensions={2}, use_global_device_ids=true | all-gather | bytes 737280 | tf_op jit(solution)/shard_map/all_gather | solution.py:202
  138.2 1.5 copy.123
  139.7 2.9 %reshape.517 = bf16[64,5120]{1,0:T(8,128)(2,1)} reshape(bf16[64,64,80]{2,1,0:T(8,128)(2,1)S(1)} %copy.123) | data formatting | bytes 1310720 | tf_op jit(solution)/shard_map/reshape | solution.py:203
  (53 shorter events, 1.3 us)
Async XLA Ops:
  6.5 43.8 %copy-start.3 = (bf16[64,128]{1,0:T(8,128)(2,1)S(1)}, bf16[64,128]{1,0:T(8,128)(2,1)}, u32[]{:S(2)}) copy-start(bf16[64,128]{1,0:T(8,128)(2,1)} %param.10) | copy-start | bytes 49156
  6.5 48.6 %copy-start.1 = (bf16[16,128,128]{2,1,0:T(8,128)(2,1)S(1)}, bf16[16,128,128]{2,1,0:T(8,128)(2,1)}, u32[]{:S(2)}) copy-start(bf16[16,128,128]{2,1,0:T(8,128)(2,1)} %param.11) | copy-start | bytes 1572868
  6.5 93.8 %all-gather.2.cloned.1.call-start = ((), (), s32[]{:S(2)}) async-start(), calls=%async_computation.1 | async-start | bytes 6963200 | tf_op jit(solution)/shard_map/all_gather | solution.py:80
  24.2 30.9 %copy-start.2 = (bf16[16,128,128]{2,1,0:T(8,128)(2,1)S(1)}, bf16[16,128,128]{2,1,0:T(8,128)(2,1)}, u32[]{:S(2)}) copy-start(bf16[16,128,128]{2,1,0:T(8,128)(2,1)} %param.12) | copy-start | bytes 1572868
  50.8 5.2 %collective-permute-start = (bf16[64,7,128]{2,1,0:T(8,128)(2,1)S(1)}, bf16[64,7,128]{2,1,0:T(8,128)(2,1)S(1)}, u32[]{:S(2)}, u32[]{:S(2)}) collective-permute-start(bf16[64,7,128]{2,1,0:T(8,128)(2,1)S(1)} %pad_maximum_fusion.1), channel_id=1, source_target_pairs={{0,8},{8,0},{1,9},{9,1},{2,10},{10,2},{3,11},{11,3},{4,12},{12,4},... | collective-permute-start | bytes 344072 | tf_op jit(solution)/shard_map/ppermute | solution.py:38
  57.1 2.2 %copy-start = (f32[128,5,1024]{2,0,1:T(8,128)}, f32[128,5,1024]{2,0,1:T(8,128)S(1)}, u32[]{:S(2)}) copy-start(f32[128,5,1024]{2,0,1:T(8,128)S(1)} %get-tuple-element.38) | copy-start | bytes 7864324
  63.5 3.4 %collective-permute-start.1 = (bf16[64,1,5,130]{3,0,2,1:T(8,128)(2,1)S(1)}, bf16[64,1,5,130]{3,0,2,1:T(8,128)(2,1)S(1)}, u32[]{:S(2)}, u32[]{:S(2)}) collective-permute-start(bf16[64,1,5,130]{3,0,2,1:T(8,128)(2,1)S(1)} %pad_maximum_fusion), channel_id=1, source_target_pairs={{0,8},{8,0},{1,9},{9,1},{2,10},{10,2},{3,11},{11,3},{4,12},{12,4},... | collective-permute-start | bytes 249608 | tf_op jit(solution)/shard_map/ppermute | solution.py:38
  67.4 7.8 %collective-permute-start.2 = (bf16[64,1,640]{2,0,1:T(8,128)(2,1)S(1)}, bf16[64,1,640]{2,0,1:T(8,128)(2,1)S(1)}, u32[]{:S(2)}, u32[]{:S(2)}) collective-permute-start(bf16[64,1,640]{2,0,1:T(8,128)(2,1)S(1)} %copy_bitcast_fusion), channel_id=1, source_target_pairs={{0,1},{1,2},{2,3},{3,4},{4,5},{5,6},{6,7},{7,0},{8,9},{9,10},{10,1... | collective-permute-start | bytes 245768 | tf_op jit(solution)/shard_map/ppermute | solution.py:28
  75.3 7.5 %collective-permute-start.3 = (bf16[64,1,640]{2,0,1:T(8,128)(2,1)S(1)}, bf16[64,1,640]{2,0,1:T(8,128)(2,1)S(1)}, u32[]{:S(2)}, u32[]{:S(2)}) collective-permute-start(bf16[64,1,640]{2,0,1:T(8,128)(2,1)S(1)} %collective-permute-done.2), channel_id=1, source_target_pairs={{0,1},{1,2},{2,3},{3,4},{4,5},{5,6},{6,7},{7,0},{8,9},{9,10},{10,1... | collective-permute-start | bytes 245768 | tf_op jit(solution)/shard_map/ppermute | solution.py:28
  77.2 7.5 %collective-permute-start.6 = (bf16[64,1,640]{2,0,1:T(8,128)(2,1)S(1)}, bf16[64,1,640]{2,0,1:T(8,128)(2,1)S(1)}, u32[]{:S(2)}, u32[]{:S(2)}) collective-permute-start(bf16[64,1,640]{2,0,1:T(8,128)(2,1)S(1)} %copy_bitcast_fusion), channel_id=1, source_target_pairs={{1,0},{2,1},{3,2},{4,3},{5,4},{6,5},{7,6},{0,7},{9,8},{10,9},{11,1... | collective-permute-start | bytes 245768 | tf_op jit(solution)/shard_map/ppermute | solution.py:30
  82.8 7.5 %collective-permute-start.4 = (bf16[64,1,640]{2,0,1:T(8,128)(2,1)S(1)}, bf16[64,1,640]{2,0,1:T(8,128)(2,1)S(1)}, u32[]{:S(2)}, u32[]{:S(2)}) collective-permute-start(bf16[64,1,640]{2,0,1:T(8,128)(2,1)S(1)} %collective-permute-done.3), channel_id=1, source_target_pairs={{0,1},{1,2},{2,3},{3,4},{4,5},{5,6},{6,7},{7,0},{8,9},{9,10},{10,1... | collective-permute-start | bytes 245768 | tf_op jit(solution)/shard_map/ppermute | solution.py:28
  84.7 7.7 %collective-permute-start.7 = (bf16[64,1,640]{2,0,1:T(8,128)(2,1)S(1)}, bf16[64,1,640]{2,0,1:T(8,128)(2,1)S(1)}, u32[]{:S(2)}, u32[]{:S(2)}) collective-permute-start(bf16[64,1,640]{2,0,1:T(8,128)(2,1)S(1)} %collective-permute-done.6), channel_id=1, source_target_pairs={{1,0},{2,1},{3,2},{4,3},{5,4},{6,5},{7,6},{0,7},{9,8},{10,9},{11,1... | collective-permute-start | bytes 245768 | tf_op jit(solution)/shard_map/ppermute | solution.py:30
  90.3 7.5 %collective-permute-start.5 = (bf16[64,1,640]{2,0,1:T(8,128)(2,1)S(1)}, bf16[64,1,640]{2,0,1:T(8,128)(2,1)S(1)}, u32[]{:S(2)}, u32[]{:S(2)}) collective-permute-start(bf16[64,1,640]{2,0,1:T(8,128)(2,1)S(1)} %collective-permute-done.4), channel_id=1, source_target_pairs={{0,1},{1,2},{2,3},{3,4},{4,5},{5,6},{6,7},{7,0},{8,9},{9,10},{10,1... | collective-permute-start | bytes 245768 | tf_op jit(solution)/shard_map/ppermute | solution.py:28
  92.5 7.2 %collective-permute-start.8 = (bf16[64,1,640]{2,0,1:T(8,128)(2,1)S(1)}, bf16[64,1,640]{2,0,1:T(8,128)(2,1)S(1)}, u32[]{:S(2)}, u32[]{:S(2)}) collective-permute-start(bf16[64,1,640]{2,0,1:T(8,128)(2,1)S(1)} %collective-permute-done.7), channel_id=1, source_target_pairs={{1,0},{2,1},{3,2},{4,3},{5,4},{6,5},{7,6},{0,7},{9,8},{10,9},{11,1... | collective-permute-start | bytes 245768 | tf_op jit(solution)/shard_map/ppermute | solution.py:30
Sparse Core Ops, SparseCore 0:
  45.6 44.2 all-gather.1
